TPU v7x, 256 devices: a whole 4x4x8 slice. The times are simulated.
256 devices in a mesh: row: 8 (over y, core), col: 16 (over x_lo, z), req: 2 (over x_hi).
Axes of the slice: x: 4 (x_hi: 2, x_lo: 2; x = x_hi * 2 + x_lo), y: 4, z: 8, core: 2. Of those that a mesh axis runs over, the one named last changes fastest.
Arguments:
- tokens: bfloat16 [3072, 4096], P(('req', 'row'), 'col'), may hold values from -6 to 6
- up_weight: bfloat16 [4096, 21504], P('col', 'row'), may hold values from -0.09375 to 0.09375
- down_weight: bfloat16 [21504, 4096], P('row', 'col'), may hold values from -0.0390625 to 0.0390625
- pool_states: float32 [192, 2, 128, 64, 128], P('row', 'req', 'col'), may hold values from -6 to 6
- pool_edges: float32 [192, 2, 128, 64, 3], P('row', 'req', 'col'), may hold values from -6 to 6
- finish_ids: int32 [32], replicated, may hold values from 0 to 191, as said below
- slot_perm: int32 [32], replicated, may hold values from 0 to 31, each once
Outputs:
- layer_out: bfloat16 [3072, 4096], P(('req', 'row'), 'col')
- decode_states: float32 [32, 2, 128, 64, 128], P('req', None, 'col', 'row')
- decode_edges: float32 [32, 2, 128, 64, 3], P('req', None, 'col', 'row')
Inputs may be any that keep to these rules, and one draw needn't show every extreme that they name: `finish_ids`: entries are distinct; of the 24 slots r * 24 to (r + 1) * 24 - 1 of one index r of row, at most 8 are named, and exactly 8 for some index. `slot_perm`: every decode slot is named once.
All inputs are finite; a program needn't handle non-finite values.
Results may differ from a plain program's by a relative error of at most 0.0044.
Values may be sent and summed in bfloat16 or wider, within the bound.
No kernel may reach another device: no remote copies, remote signals or barrier semaphores. Data moves between devices by JAX's collectives and lax.ppermute only.
A program may use at most 128 MiB of HBM per device.

v0:
```python
import jax
import jax.numpy as jnp
from jax import lax
from jax.sharding import PartitionSpec as P


def handover(pool_states, pool_edges, finish_ids, slot_perm):
    finished = slot_perm.shape[0]
    numbers = jnp.arange(finished, dtype=jnp.int32)
    matches = slot_perm[None, :] == numbers[:, None]
    inverse = jnp.sum(jnp.where(matches, numbers[None, :], 0), axis=1)
    arrived = (
        lax.all_to_all(pool_states, "row", split_axis=3, concat_axis=0, tiled=True),
        lax.all_to_all(pool_edges, "row", split_axis=3, concat_axis=0, tiled=True),
    )
    wanted_rows = finish_ids[inverse]
    states = arrived[0][wanted_rows]
    edge_rows = arrived[1][wanted_rows]
    return (
        lax.all_to_all(states, "req", split_axis=0, concat_axis=1, tiled=True),
        lax.all_to_all(edge_rows, "req", split_axis=0, concat_axis=1, tiled=True),
    )


def on_device(tokens, up_weight, down_weight, pool_states, pool_edges, finish_ids, slot_perm):
    gathered = lax.all_gather(tokens, "row", axis=0, tiled=True)
    preact = lax.psum_scatter(
        jnp.dot(gathered, up_weight, preferred_element_type=jnp.float32),
        "col",
        scatter_dimension=0,
        tiled=True,
    )
    active = jnp.maximum(preact, 0.0)
    hidden = (active * active).astype(jnp.bfloat16)
    products = jnp.dot(
        lax.all_gather(hidden, "col", axis=0, tiled=True),
        down_weight,
        preferred_element_type=jnp.float32,
    )
    summed = lax.psum_scatter(products, "row", scatter_dimension=0, tiled=True)
    layer_out = (tokens.astype(jnp.float32) + summed).astype(jnp.bfloat16)
    decode_states, decode_edges = handover(pool_states, pool_edges, finish_ids, slot_perm)
    return (layer_out, decode_states, decode_edges)


def solution(mesh):
    in_specs = (
        P(("req", "row"), "col"),
        P("col", "row"),
        P("row", "col"),
        P("row", "req", "col", None, None),
        P("row", "req", "col", None, None),
        P(),
        P(),
    )
    out_specs = (
        P(("req", "row"), "col"),
        P("req", None, "col", "row", None),
        P("req", None, "col", "row", None),
    )
    return jax.shard_map(
        on_device, mesh=mesh, in_specs=in_specs, out_specs=out_specs, check_vma=False
    )
```

profile of v0, /device:TPU:8, one launch (start us, length us, event | category | flops | bytes accessed | tf_op | source)
XLA Modules:
  0.0 376.9 jit_solution(2078895432324157047)
XLA Ops:
  7.2 0.0 copy-start
  7.2 0.0 reduce-scatter.3.cloned.1.call-start
  7.2 14.0 %all_gather.6 = bf16[1536,256]{1,0:T(8,128)(2,1)S(1)} all-gather(bf16[192,256]{1,0:T(8,128)(2,1)} %param.7), channel_id=1, replica_groups=mesh['row'=8,'col'=16,'req'=2] {'row'}, dimensions={0}, use_global_device_ids=true | all-gather | bytes 884736 | tf_op jit(solution)/shard_map/all_gather | solution.py:26
  21.2 0.0 copy-done
  21.2 8.1 %fusion.2 = f32[1536,2688]{1,0:T(8,128)} fusion(bf16[1536,256]{1,0:T(8,128)(2,1)S(1)} %all_gather.6, bf16[256,2688]{1,0:T(8,128)(2,1)S(1)} %copy-done), kind=kOutput, calls=%fused_computation.16 | convolution fusion | flops 2113929216 | bytes 18677760 | tf_op jit(solution)/shard_map/dot_general | solution.py:28
  29.3 0.0 reduce-scatter.3.cloned.1.call-update
  29.3 0.0 all-gather.2.cloned.1.call-start
  29.3 185.7 %reduce-scatter.3.cloned.1.call-done = f32[96,2688]{1,0:T(8,128)} async-done(((f32[1536,2688]{1,0:T(8,128)}), f32[96,2688]{1,0:T(8,128)}) %reduce-scatter.3.cloned.1.call-update) | async-done | bytes 1032208 | tf_op jit(solution)/shard_map/reduce_scatter | solution.py:27
  215.0 2.1 multiply_convert_fusion
  217.1 0.0 all-gather.2.cloned.1.call-update
  217.1 0.0 copy-done.4
  217.1 0.3 copy.50
  217.4 1.2 reshape.63
  218.7 4.8 %all-to-all-start.2 = ((f32[8,1,4608]{2,1,0:T(1,128)}), f32[8,1,4608]{2,1,0:T(1,128)S(1)}, u32[]{:S(2)}, u32[]{:S(2)}) async-start(f32[8,1,4608]{2,1,0:T(1,128)} %reshape.63), calls=%async_computation.4 | async-start | bytes 294912 | tf_op jit(solution)/shard_map/all_to_all | solution.py:14
  223.5 9.0 %copy.46 = f32[24,1,8,64,128]{4,2,0,1,3:T(8,128)} copy(f32[24,1,8,64,128]{4,3,2,1,0:T(8,128)} %param.10) | data formatting | bytes 12582912 | tf_op args[3]
  232.5 0.0 all-to-all-done.2
  232.5 4.9 %all-to-all-start = ((f32[24,1,8,64,128]{4,2,0,1,3:T(8,128)}), f32[24,1,8,64,128]{4,2,0,1,3:T(8,128)}, u32[]{:S(2)}, u32[]{:S(2)}) async-start(f32[24,1,8,64,128]{4,2,0,1,3:T(8,128)} %copy.46), calls=%async_computation.2 | async-start | bytes 12582912 | tf_op jit(solution)/shard_map/all_to_all | solution.py:13
  237.5 0.2 reduce-scatter.5.cloned.1.call-start
  237.7 77.0 %all-gather.2.cloned.1.call-done = bf16[1536,2688]{1,0:T(8,128)(2,1)} async-done(((bf16[96,2688]{1,0:T(8,128)(2,1)}), bf16[1536,2688]{1,0:T(8,128)(2,1)}) %all-gather.2.cloned.1.call-update) | async-done | bytes 8257552 | tf_op jit(solution)/shard_map/all_gather | solution.py:36
  314.7 0.0 copy-done.5
  314.7 6.9 %fusion.3 = f32[1536,256]{1,0:T(8,128)} fusion(bf16[1536,2688]{1,0:T(8,128)(2,1)} %all-gather.2.cloned.1.call-done, bf16[2688,256]{1,0:T(8,128)(2,1)S(1)} %copy-done.5), kind=kOutput, calls=%fused_computation.17 | convolution fusion | flops 2113929216 | bytes 11206656 | tf_op jit(solution)/shard_map/dot_general | solution.py:35
  321.7 0.0 reduce-scatter.5.cloned.1.call-update
  321.7 0.0 copy-done.6
  321.7 0.1 select_reduce_fusion
  321.8 0.0 copy-done.2
  321.9 0.7 gather_fusion
  322.6 0.5 broadcast.50
  323.1 1.0 reduce
  324.1 0.5 reshape.64
  324.6 0.2 copy.64
  324.8 2.1 copy.58
  326.9 2.2 gather_fusion.2
  329.2 0.8 reshape.65
  330.0 0.0 all-to-all-done
  330.0 4.0 %all-to-all-start.3 = ((f32[2,1,3072]{2,1,0:T(1,128)}), f32[2,1,3072]{2,1,0:T(1,128)S(1)}, u32[]{:S(2)}, u32[]{:S(2)}) async-start(f32[2,1,3072]{2,1,0:T(1,128)} %reshape.65), calls=%async_computation.5 | async-start | bytes 49152 | tf_op jit(solution)/shard_map/all_to_all | solution.py:21
  334.0 6.5 %copy.63 = f32[24,1,8,64,128]{4,3,2,0,1:T(8,128)S(1)} copy(f32[24,1,8,64,128]{4,2,0,1,3:T(8,128)} %all-to-all-done) | data formatting | bytes 12582912 | tf_op jit(solution)/shard_map/all_to_all | solution.py:13
  340.4 0.0 copy-start.1
  340.5 3.6 copy.48
  344.0 4.5 %gather_fusion.1 = f32[32,8,8,128]{3,2,1,0:T(8,128)} fusion(f32[192,8,8,128]{3,2,1,0:T(8,128)} %bitcast.46, s32[1024]{0:T(1024)S(1)} %pad_clamp_fusion), kind=kCustom, calls=%fused_computation.1 | custom fusion | bytes 2097280 | tf_op jit(solution)/shard_map/gather | solution.py:17
  348.5 0.0 all-to-all-done.3
  348.5 4.8 %all-to-all-start.1 = ((f32[32,1,8,8,128]{4,3,2,1,0:T(8,128)}), f32[32,1,8,8,128]{4,3,2,1,0:T(8,128)S(1)}, u32[]{:S(2)}, u32[]{:S(2)}) async-start(f32[32,1,8,8,128]{4,3,2,1,0:T(8,128)} %bitcast.8), calls=%async_computation.3 | async-start | bytes 2097152 | tf_op jit(solution)/shard_map/all_to_all | solution.py:20
  353.3 0.7 reduce.1
  354.0 0.2 reshape.66
  354.3 0.2 copy.59
  354.5 0.7 copy.57
  355.2 12.5 %all-to-all-done.1 = f32[32,1,8,8,128]{4,3,2,1,0:T(8,128)S(1)} async-done(((f32[32,1,8,8,128]{4,3,2,1,0:T(8,128)}), f32[32,1,8,8,128]{4,3,2,1,0:T(8,128)S(1)}, u32[]{:S(2)}, u32[]{:S(2)}) %all-to-all-start.1) | async-done | bytes 1048608 | tf_op jit(solution)/shard_map/all_to_all | solution.py:20
  367.7 1.0 copy.56
  368.8 1.6 add_convert_fusion
  (13 shorter events, 0.1 us)
Async XLA Ops:
  7.2 14.0 %copy-start = (bf16[256,2688]{1,0:T(8,128)(2,1)S(1)}, bf16[256,2688]{1,0:T(8,128)(2,1)}, u32[]{:S(2)}) copy-start(bf16[256,2688]{1,0:T(8,128)(2,1)} %param.8) | copy-start | bytes 4128772
  7.2 207.8 %reduce-scatter.3.cloned.1.call-start = ((), (), s32[]{:S(2)}) async-start(), calls=%async_computation.6 | async-start | bytes 17547264 | tf_op jit(solution)/shard_map/reduce_scatter | solution.py:27
  29.3 187.8 %copy-start.4 = (f32[24,1,8,64,3]{3,2,4,1,0:T(8,128)S(1)}, f32[24,1,8,64,3]{3,2,4,1,0:T(8,128)}, u32[]{:S(2)}) copy-start(f32[24,1,8,64,3]{3,2,4,1,0:T(8,128)} %param.11) | copy-start | bytes 442372
  29.3 285.4 %all-gather.2.cloned.1.call-start = ((), (), s32[]{:S(2)}) async-start(), calls=%async_computation.7 | async-start | bytes 8773632 | tf_op jit(solution)/shard_map/all_gather | solution.py:36
  218.7 13.8 %all-to-all-start.2 = ((f32[8,1,4608]{2,1,0:T(1,128)}), f32[8,1,4608]{2,1,0:T(1,128)S(1)}, u32[]{:S(2)}, u32[]{:S(2)}) async-start(f32[8,1,4608]{2,1,0:T(1,128)} %reshape.63), calls=%async_computation.4 | async-start | bytes 294912 | tf_op jit(solution)/shard_map/all_to_all | solution.py:14
  232.5 82.2 %copy-start.5 = (bf16[2688,256]{1,0:T(8,128)(2,1)S(1)}, bf16[2688,256]{1,0:T(8,128)(2,1)}, u32[]{:S(2)}) copy-start(bf16[2688,256]{1,0:T(8,128)(2,1)} %param.9) | copy-start | bytes 4128772
  232.5 97.5 %all-to-all-start = ((f32[24,1,8,64,128]{4,2,0,1,3:T(8,128)}), f32[24,1,8,64,128]{4,2,0,1,3:T(8,128)}, u32[]{:S(2)}, u32[]{:S(2)}) async-start(f32[24,1,8,64,128]{4,2,0,1,3:T(8,128)} %copy.46), calls=%async_computation.2 | async-start | bytes 12582912 | tf_op jit(solution)/shard_map/all_to_all | solution.py:13
  237.5 84.2 %copy-start.6 = (s32[32]{0:T(128)S(1)}, s32[32]{0:T(128)}, u32[]{:S(2)}) copy-start(s32[32]{0:T(128)} %param.13) | copy-start | bytes 388
  237.5 84.4 %copy-start.2 = (s32[32]{0:T(128)S(1)}, s32[32]{0:T(128)}, u32[]{:S(2)}) copy-start(s32[32]{0:T(128)} %param.12) | copy-start | bytes 388
  237.5 131.3 %reduce-scatter.5.cloned.1.call-start = ((), (), s32[]{:S(2)}) async-start(), calls=%async_computation.8 | async-start | bytes 1769472 | tf_op jit(solution)/shard_map/reduce_scatter | solution.py:40
  330.0 18.5 %all-to-all-start.3 = ((f32[2,1,3072]{2,1,0:T(1,128)}), f32[2,1,3072]{2,1,0:T(1,128)S(1)}, u32[]{:S(2)}, u32[]{:S(2)}) async-start(f32[2,1,3072]{2,1,0:T(1,128)} %reshape.65), calls=%async_computation.5 | async-start | bytes 49152 | tf_op jit(solution)/shard_map/all_to_all | solution.py:21
  340.4 29.9 %copy-start.1 = (bf16[256,2688]{1,0:T(8,128)(2,1)S(1)}, bf16[256,2688]{1,0:T(8,128)(2,1)}, u32[]{:S(2)}) copy-start(bf16[256,2688]{1,0:T(8,128)(2,1)} %param.8) | copy-start | bytes 4128772
  344.0 24.7 %copy-start.3 = (bf16[192,256]{1,0:T(8,128)(2,1)S(1)}, bf16[192,256]{1,0:T(8,128)(2,1)}, u32[]{:S(2)}) copy-start(bf16[192,256]{1,0:T(8,128)(2,1)} %param.7) | copy-start | bytes 294916
  348.5 19.2 %all-to-all-start.1 = ((f32[32,1,8,8,128]{4,3,2,1,0:T(8,128)}), f32[32,1,8,8,128]{4,3,2,1,0:T(8,128)S(1)}, u32[]{:S(2)}, u32[]{:S(2)}) async-start(f32[32,1,8,8,128]{4,3,2,1,0:T(8,128)} %bitcast.8), calls=%async_computation.3 | async-start | bytes 2097152 | tf_op jit(solution)/shard_map/all_to_all | solution.py:20
Sparse Core Ops, SparseCore 0:
  29.4 185.5 reduce-scatter.2
  217.4 97.3 all-gather.1
  321.8 30.1 reduce-scatter.4
where the time goes:
time: 378 us; the launch traced here: 377 us
  waiting for transfers between devices  275 us (73%)
  local copies, waits for them, and re-layouts  34.4 us (9%)
  starting transfers between devices  18.8 us (5%)
  matrix products  15 us (4%)
  blocking collectives  14 us (4%)
  between operations  13.9 us (4%)
  other arithmetic  5.52 us (1%)
    reduce_scatter x1, waiting for transfers between devices, on_device(): lax.psum_scatter(jnp.dot(gathered, up_weight, preferred_element_type=jnp....  186 us
    all_gather x1, waiting for transfers between devices, on_device(): lax.all_gather(hidden, 'col', axis=0, tiled=True)  77 us
    unnamed x23, local copies, waits for them, and re-layouts  14 us
    all_gather x1, blocking collectives, on_device(): gathered = lax.all_gather(tokens, 'row', axis=0, tiled=True)  14 us
    all_to_all x1, waiting for transfers between devices, handover(): lax.all_to_all(states, 'req', split_axis=0, concat_axis=1, tiled=True)  12.5 us
    all_to_all x2, local copies, waits for them, and re-layouts, handover(): lax.all_to_all(pool_states, 'row', split_axis=3, concat_axis=0, tiled=True)  10 us
    dot_general x1, matrix products, on_device(): jnp.dot(gathered, up_weight, preferred_element_type=jnp.float32)  8.06 us
  transfers between devices with their start and end apart: 7, of which 3 were waited for; matrix products, arithmetic and copies ran while one was open for 11% of the time, Pallas kernels for 0%

commit v1 on v0

--- a/solution.py
+++ b/solution.py
@@ -2,6 +2,29 @@
 import jax.numpy as jnp
 from jax import lax
 from jax.sharding import PartitionSpec as P
+
+
+def split_up(x, dim, size):
+    shape = x.shape
+    blocks = x.reshape(*shape[:dim], size, shape[dim] // size, *shape[dim + 1 :])
+    return jnp.moveaxis(blocks, dim, 0)
+
+
+def in_order(blocks, dim):
+    blocks = jnp.moveaxis(blocks, 0, dim)
+    shape = blocks.shape
+    return blocks.reshape(*shape[:dim], shape[dim] * shape[dim + 1], *shape[dim + 2 :])
+
+
+def swapped_with_each(x, axis, split_dim, concat_dim):
+    size, index = (lax.axis_size(axis), lax.axis_index(axis))
+    parts = split_up(x, split_dim, size)
+    finished = [parts[index]]
+    for hop in range(1, size):
+        sent = parts[index ^ hop]
+        finished.append(lax.ppermute(sent, axis, [(i, i ^ hop) for i in range(size)]))
+    parts = jnp.stack(finished)[index ^ jnp.arange(size)]
+    return in_order(parts, concat_dim)
 
 
 def handover(pool_states, pool_edges, finish_ids, slot_perm):
@@ -11,7 +34,7 @@
     inverse = jnp.sum(jnp.where(matches, numbers[None, :], 0), axis=1)
     arrived = (
         lax.all_to_all(pool_states, "row", split_axis=3, concat_axis=0, tiled=True),
-        lax.all_to_all(pool_edges, "row", split_axis=3, concat_axis=0, tiled=True),
+        swapped_with_each(pool_edges, "row", 3, 0),
     )
     wanted_rows = finish_ids[inverse]
     states = arrived[0][wanted_rows]

time: 378 us -> 384 us (1.016)
  waiting for transfers between devices: 275 us -> 281 us
    ppermute x0 -> x7, starting transfers between devices: none -> 6.87 us  [swapped_with_each(): lax.ppermute(sent, axis, [(i, i ^ hop) for i in range(size)])]
    ppermute x0 -> x7, waiting for transfers between devices: none -> 4.98 us  [swapped_with_each(): lax.ppermute(sent, axis, [(i, i ^ hop) for i in range(size)])]
    all_to_all x1 -> x0, starting transfers between devices: 4.83 us -> none  [handover(): lax.all_to_all(pool_edges, 'row', split_axis=3, concat_axis=0, tiled=True)]
    unnamed x23 -> x26, local copies, waits for them, and re-layouts: 14 us -> 12.2 us
  transfers between devices with their start and end apart: 7 -> 13, of which waited for: 3 -> 5; matrix products, arithmetic and copies ran while one was open for 11% -> 11% of each run, Pallas kernels for 0% -> 0%
where the time goes in v1:
time: 384 us; the launch traced here: 383 us
  waiting for transfers between devices  281 us (73%)
  local copies, waits for them, and re-layouts  33.3 us (9%)
  starting transfers between devices  21.1 us (5%)
  matrix products  15.3 us (4%)
  blocking collectives  14 us (4%)
  between operations  14 us (4%)
  other arithmetic  4.53 us (1%)
    reduce_scatter x1, waiting for transfers between devices, on_device(): lax.psum_scatter(jnp.dot(gathered, up_weight, preferred_element_type=jnp....  186 us
    all_gather x1, waiting for transfers between devices, on_device(): lax.all_gather(hidden, 'col', axis=0, tiled=True)  77.5 us
    all_gather x1, blocking collectives, on_device(): gathered = lax.all_gather(tokens, 'row', axis=0, tiled=True)  14 us
    all_to_all x1, waiting for transfers between devices, handover(): lax.all_to_all(states, 'req', split_axis=0, concat_axis=1, tiled=True)  12.4 us
    unnamed x26, local copies, waits for them, and re-layouts  12.2 us
    all_to_all x2, local copies, waits for them, and re-layouts, handover(): lax.all_to_all(pool_states, 'row', split_axis=3, concat_axis=0, tiled=True)  10 us
    dot_general x1, matrix products, on_device(): jnp.dot(gathered, up_weight, preferred_element_type=jnp.float32)  8.06 us
  transfers between devices with their start and end apart: 13, of which 5 were waited for; matrix products, arithmetic and copies ran while one was open for 11% of the time, Pallas kernels for 0%

profile of v1, /device:TPU:8, one launch (start us, length us, event | category | flops | bytes accessed | tf_op | source)
XLA Modules:
  0.0 382.8 jit_solution(3809981221154289801)
XLA Ops:
  7.2 0.0 copy-start
  7.2 0.0 reduce-scatter.3.cloned.1.call-start
  7.2 14.0 %all_gather.6 = bf16[1536,256]{1,0:T(8,128)(2,1)S(1)} all-gather(bf16[192,256]{1,0:T(8,128)(2,1)} %param.7), channel_id=1, replica_groups=mesh['row'=8,'col'=16,'req'=2] {'row'}, dimensions={0}, use_global_device_ids=true | all-gather | bytes 884736 | tf_op jit(solution)/shard_map/all_gather | solution.py:49
  21.2 8.1 %fusion.3 = f32[1536,2688]{1,0:T(8,128)} fusion(bf16[1536,256]{1,0:T(8,128)(2,1)S(1)} %all_gather.6, bf16[256,2688]{1,0:T(8,128)(2,1)S(1)} %copy-done), kind=kOutput, calls=%fused_computation.34 | convolution fusion | flops 2113929216 | bytes 18677760 | tf_op jit(solution)/shard_map/dot_general | solution.py:51
  29.3 0.0 reduce-scatter.3.cloned.1.call-update
  29.3 0.0 all-gather.2.cloned.1.call-start
  29.3 185.7 %reduce-scatter.3.cloned.1.call-done = f32[96,2688]{1,0:T(8,128)} async-done(((f32[1536,2688]{1,0:T(8,128)}), f32[96,2688]{1,0:T(8,128)}) %reduce-scatter.3.cloned.1.call-update) | async-done | bytes 1032208 | tf_op jit(solution)/shard_map/reduce_scatter | solution.py:50
  215.0 2.1 multiply_convert_fusion
  217.1 0.0 all-gather.2.cloned.1.call-update
  217.1 9.0 %copy.39 = f32[24,1,8,64,128]{4,2,0,1,3:T(8,128)} copy(f32[24,1,8,64,128]{4,3,2,1,0:T(8,128)} %param.10) | data formatting | bytes 12582912 | tf_op args[3]
  226.1 5.4 %all-to-all-start = ((f32[24,1,8,64,128]{4,2,0,1,3:T(8,128)}), f32[24,1,8,64,128]{4,2,0,1,3:T(8,128)}, u32[]{:S(2)}, u32[]{:S(2)}) async-start(f32[24,1,8,64,128]{4,2,0,1,3:T(8,128)} %copy.39), calls=%async_computation.2 | async-start | bytes 12582912 | tf_op jit(solution)/shard_map/all_to_all | solution.py:36
  231.5 0.3 copy.43
  231.8 0.1 dynamic-slice_bitcast_fusion
  231.9 0.2 collective-permute-start
  232.1 0.4 collective-permute-start.1
  232.5 1.4 collective-permute-start.2
  233.9 2.1 collective-permute-start.3
  236.0 1.2 collective-permute-start.4
  237.1 0.1 select_reduce_fusion
  237.2 0.0 copy-start.2
  237.3 77.5 %all-gather.2.cloned.1.call-done = bf16[1536,2688]{1,0:T(8,128)(2,1)} async-done(((bf16[96,2688]{1,0:T(8,128)(2,1)}), bf16[1536,2688]{1,0:T(8,128)(2,1)}) %all-gather.2.cloned.1.call-update) | async-done | bytes 8257552 | tf_op jit(solution)/shard_map/all_gather | solution.py:59
  314.7 7.3 %fusion.4 = f32[1536,256]{1,0:T(8,128)} fusion(bf16[1536,2688]{1,0:T(8,128)(2,1)} %all-gather.2.cloned.1.call-done, bf16[2688,256]{1,0:T(8,128)(2,1)} %param.9), kind=kOutput, calls=%fused_computation.35 | convolution fusion | flops 2113929216 | bytes 11206656 | tf_op jit(solution)/shard_map/dot_general | solution.py:58
  322.0 0.0 reduce-scatter.5.cloned.1.call-update
  322.1 0.7 gather_fusion
  322.8 0.0 collective-permute-done
  322.8 1.6 collective-permute-start.5
  324.4 0.0 collective-permute-done.1
  324.4 0.1 collective-permute-start.6
  324.6 2.9 collective-permute-done.5
  327.6 2.0 collective-permute-done.6
  329.6 0.6 gather_fusion.2
  330.2 2.1 copy.50
  332.4 2.3 gather_fusion.3
  334.7 0.8 reshape.113
  335.5 3.9 %all-to-all-start.2 = ((f32[2,1,3072]{2,1,0:T(1,128)}), f32[2,1,3072]{2,1,0:T(1,128)S(1)}, u32[]{:S(2)}, u32[]{:S(2)}) async-start(f32[2,1,3072]{2,1,0:T(1,128)} %reshape.113), calls=%async_computation.4 | async-start | bytes 49152 | tf_op jit(solution)/shard_map/all_to_all | solution.py:44
  339.5 6.5 %copy.54 = f32[24,1,8,64,128]{4,3,2,0,1:T(8,128)S(1)} copy(f32[24,1,8,64,128]{4,2,0,1,3:T(8,128)} %all-to-all-done) | data formatting | bytes 12582912 | tf_op jit(solution)/shard_map/all_to_all | solution.py:36
  345.9 0.0 copy-start.1
  345.9 3.6 copy.41
  349.5 4.4 %gather_fusion.1 = f32[32,8,8,128]{3,2,1,0:T(8,128)} fusion(f32[192,8,8,128]{3,2,1,0:T(8,128)} %bitcast.74, s32[1024]{0:T(1024)S(1)} %pad_clamp_fusion.1), kind=kCustom, calls=%fused_computation.1 | custom fusion | bytes 2097280 | tf_op jit(solution)/shard_map/gather | solution.py:40
  353.9 4.8 %all-to-all-start.1 = ((f32[32,1,8,8,128]{4,3,2,1,0:T(8,128)}), f32[32,1,8,8,128]{4,3,2,1,0:T(8,128)S(1)}, u32[]{:S(2)}, u32[]{:S(2)}) async-start(f32[32,1,8,8,128]{4,3,2,1,0:T(8,128)} %bitcast.8), calls=%async_computation.3 | async-start | bytes 2097152 | tf_op jit(solution)/shard_map/all_to_all | solution.py:43
  358.8 0.5 broadcast.85
  359.3 0.7 reduce
  360.0 0.2 reshape.114
  360.2 0.2 copy.51
  360.5 0.7 copy.49
  361.2 12.4 %all-to-all-done.1 = f32[32,1,8,8,128]{4,3,2,1,0:T(8,128)S(1)} async-done(((f32[32,1,8,8,128]{4,3,2,1,0:T(8,128)}), f32[32,1,8,8,128]{4,3,2,1,0:T(8,128)S(1)}, u32[]{:S(2)}, u32[]{:S(2)}) %all-to-all-start.1) | async-done | bytes 1048608 | tf_op jit(solution)/shard_map/all_to_all | solution.py:43
  373.6 1.0 copy.48
  374.6 1.6 add_convert_fusion
  (31 shorter events, 0.2 us)
Async XLA Ops:
  7.2 14.0 %copy-start = (bf16[256,2688]{1,0:T(8,128)(2,1)S(1)}, bf16[256,2688]{1,0:T(8,128)(2,1)}, u32[]{:S(2)}) copy-start(bf16[256,2688]{1,0:T(8,128)(2,1)} %param.8) | copy-start | bytes 4128772
  7.2 207.8 %reduce-scatter.3.cloned.1.call-start = ((), (), s32[]{:S(2)}) async-start(), calls=%async_computation.5 | async-start | bytes 17547264 | tf_op jit(solution)/shard_map/reduce_scatter | solution.py:50
  29.3 285.4 %all-gather.2.cloned.1.call-start = ((), (), s32[]{:S(2)}) async-start(), calls=%async_computation.6 | async-start | bytes 8773632 | tf_op jit(solution)/shard_map/all_gather | solution.py:59
  226.1 5.4 %copy-start.4 = (f32[24,1,8,64,3]{3,2,4,1,0:T(8,128)S(1)}, f32[24,1,8,64,3]{3,2,4,1,0:T(8,128)}, u32[]{:S(2)}) copy-start(f32[24,1,8,64,3]{3,2,4,1,0:T(8,128)} %param.11) | copy-start | bytes 442372
  226.1 11.0 %copy-start.5 = (s32[32]{0:T(128)S(1)}, s32[32]{0:T(128)}, u32[]{:S(2)}) copy-start(s32[32]{0:T(128)} %param.13) | copy-start | bytes 388
  226.1 109.4 %all-to-all-start = ((f32[24,1,8,64,128]{4,2,0,1,3:T(8,128)}), f32[24,1,8,64,128]{4,2,0,1,3:T(8,128)}, u32[]{:S(2)}, u32[]{:S(2)}) async-start(f32[24,1,8,64,128]{4,2,0,1,3:T(8,128)} %copy.39), calls=%async_computation.2 | async-start | bytes 12582912 | tf_op jit(solution)/shard_map/all_to_all | solution.py:36
  231.5 143.2 %reduce-scatter.5.cloned.1.call-start = ((), (), s32[]{:S(2)}) async-start(), calls=%async_computation.7 | async-start | bytes 1769472 | tf_op jit(solution)/shard_map/reduce_scatter | solution.py:63
  231.9 90.9 %collective-permute-start = (f32[24,1,8,8,3]{0,3,4,2,1:T(8,128)S(1)}, f32[24,1,8,8,3]{0,3,4,2,1:T(8,128)S(1)}, u32[]{:S(2)}, u32[]{:S(2)}) collective-permute-start(f32[24,1,8,8,3]{0,3,4,2,1:T(8,128)S(1)} %get-tuple-element.24), channel_id=1, source_target_pairs={{0,32},{32,0},{64,96},{96,64},{128,160},{160,128},{192,224},{224,1... | collective-permute-start | bytes 55304 | tf_op jit(solution)/shard_map/ppermute | solution.py:25
  232.1 92.3 %collective-permute-start.1 = (f32[24,1,8,8,3]{0,3,4,2,1:T(8,128)S(1)}, f32[24,1,8,8,3]{0,3,4,2,1:T(8,128)S(1)}, u32[]{:S(2)}, u32[]{:S(2)}) collective-permute-start(f32[24,1,8,8,3]{0,3,4,2,1:T(8,128)S(1)} %get-tuple-element.23), channel_id=1, source_target_pairs={{0,64},{32,96},{64,0},{96,32},{128,192},{160,224},{192,128},{224,1... | collective-permute-start | bytes 55304 | tf_op jit(solution)/shard_map/ppermute | solution.py:25
  232.5 92.0 %collective-permute-start.2 = (f32[24,1,8,8,3]{0,3,4,2,1:T(8,128)S(1)}, f32[24,1,8,8,3]{0,3,4,2,1:T(8,128)S(1)}, u32[]{:S(2)}, u32[]{:S(2)}) collective-permute-start(f32[24,1,8,8,3]{0,3,4,2,1:T(8,128)S(1)} %get-tuple-element.22), channel_id=1, source_target_pairs={{0,96},{32,64},{64,32},{96,0},{128,224},{160,192},{192,160},{224,1... | collective-permute-start | bytes 55304 | tf_op jit(solution)/shard_map/ppermute | solution.py:25
  233.9 90.7 %collective-permute-start.3 = (f32[24,1,8,8,3]{0,3,4,2,1:T(8,128)S(1)}, f32[24,1,8,8,3]{0,3,4,2,1:T(8,128)S(1)}, u32[]{:S(2)}, u32[]{:S(2)}) collective-permute-start(f32[24,1,8,8,3]{0,3,4,2,1:T(8,128)S(1)} %get-tuple-element.21), channel_id=1, source_target_pairs={{0,128},{32,160},{64,192},{96,224},{128,0},{160,32},{192,64},{224,... | collective-permute-start | bytes 55304 | tf_op jit(solution)/shard_map/ppermute | solution.py:25
  236.0 88.7 %collective-permute-start.4 = (f32[24,1,8,8,3]{0,3,4,2,1:T(8,128)S(1)}, f32[24,1,8,8,3]{0,3,4,2,1:T(8,128)S(1)}, u32[]{:S(2)}, u32[]{:S(2)}) collective-permute-start(f32[24,1,8,8,3]{0,3,4,2,1:T(8,128)S(1)} %get-tuple-element.20), channel_id=1, source_target_pairs={{0,160},{32,128},{64,224},{96,192},{128,32},{160,0},{192,96},{224,... | collective-permute-start | bytes 55304 | tf_op jit(solution)/shard_map/ppermute | solution.py:25
  237.2 84.8 %copy-start.2 = (s32[32]{0:T(128)S(1)}, s32[32]{0:T(128)}, u32[]{:S(2)}) copy-start(s32[32]{0:T(128)} %param.12) | copy-start | bytes 388
  322.8 4.7 %collective-permute-start.5 = (f32[24,1,8,8,3]{0,3,4,2,1:T(8,128)S(1)}, f32[24,1,8,8,3]{0,3,4,2,1:T(8,128)S(1)}, u32[]{:S(2)}, u32[]{:S(2)}) collective-permute-start(f32[24,1,8,8,3]{0,3,4,2,1:T(8,128)S(1)} %get-tuple-element.19), channel_id=1, source_target_pairs={{0,192},{32,224},{64,128},{96,160},{128,64},{160,96},{192,0},{224,... | collective-permute-start | bytes 55304 | tf_op jit(solution)/shard_map/ppermute | solution.py:25
  324.4 5.2 %collective-permute-start.6 = (f32[24,1,8,8,3]{0,3,4,2,1:T(8,128)S(1)}, f32[24,1,8,8,3]{0,3,4,2,1:T(8,128)S(1)}, u32[]{:S(2)}, u32[]{:S(2)}) collective-permute-start(f32[24,1,8,8,3]{0,3,4,2,1:T(8,128)S(1)} %get-tuple-element.18), channel_id=1, source_target_pairs={{0,224},{32,192},{64,160},{96,128},{128,96},{160,64},{192,32},{224... | collective-permute-start | bytes 55304 | tf_op jit(solution)/shard_map/ppermute | solution.py:25
  335.5 18.4 %all-to-all-start.2 = ((f32[2,1,3072]{2,1,0:T(1,128)}), f32[2,1,3072]{2,1,0:T(1,128)S(1)}, u32[]{:S(2)}, u32[]{:S(2)}) async-start(f32[2,1,3072]{2,1,0:T(1,128)} %reshape.113), calls=%async_computation.4 | async-start | bytes 49152 | tf_op jit(solution)/shard_map/all_to_all | solution.py:44
  345.9 30.3 %copy-start.1 = (bf16[256,2688]{1,0:T(8,128)(2,1)S(1)}, bf16[256,2688]{1,0:T(8,128)(2,1)}, u32[]{:S(2)}) copy-start(bf16[256,2688]{1,0:T(8,128)(2,1)} %param.8) | copy-start | bytes 4128772
  349.5 25.2 %copy-start.3 = (bf16[192,256]{1,0:T(8,128)(2,1)S(1)}, bf16[192,256]{1,0:T(8,128)(2,1)}, u32[]{:S(2)}) copy-start(bf16[192,256]{1,0:T(8,128)(2,1)} %param.7) | copy-start | bytes 294916
  353.9 19.7 %all-to-all-start.1 = ((f32[32,1,8,8,128]{4,3,2,1,0:T(8,128)}), f32[32,1,8,8,128]{4,3,2,1,0:T(8,128)S(1)}, u32[]{:S(2)}, u32[]{:S(2)}) async-start(f32[32,1,8,8,128]{4,3,2,1,0:T(8,128)} %bitcast.8), calls=%async_computation.3 | async-start | bytes 2097152 | tf_op jit(solution)/shard_map/all_to_all | solution.py:43
Sparse Core Ops, SparseCore 0:
  29.4 185.5 reduce-scatter.2
  217.3 97.3 all-gather.1
  322.2 30.1 reduce-scatter.4
